TPU v7x, 256 devices: a whole 4x4x8 slice. The times are simulated.
256 devices in a mesh: dp: 32 (over z, x), mp: 8 (over y, core).
Axes of the slice: x: 4, y: 4, z: 8, core: 2. Of those that a mesh axis runs over, the one named last changes fastest.
Arguments:
- token_ids: int32 [2048, 7], replicated, may hold values from 0 to 65535
- lengths: int32 [2048], replicated, may hold values from 1 to 7, as said below
- pack_dest: int32 [2048], replicated, may hold values from 0 to 31, as said below
- ref_hidden: bfloat16 [2048, 7, 4096], P('dp', None, 'mp'), may hold values from -45 to 45
- reward_hidden: bfloat16 [2048, 7, 4096], P('dp', None, 'mp'), may hold values from -140 to 140
- head_weight: bfloat16 [4096, 65536], P('mp', 'dp'), may hold values from -0.25 to 0.25
- norm_gain: float32 [4096], P('mp'), may hold values from 0.1 to 1.9
- score_weight: float32 [4096], P('mp'), may hold values from -0.09375 to 0.09375
- value_weight: float32 [4096], P('mp'), may hold values from -0.09375 to 0.09375
- old_logprob: float32 [8192], P('dp'), may hold values from -14 to -1
Outputs:
- ref_logprob: float32 [8192], P('dp')
- advantage: float32 [8192], P('dp')
Inputs may be any that keep to these rules, and one draw needn't show every extreme that they name: `pack_dest`: request i belongs to request shard i // 64. Each request shard sends exactly 2 of its requests to every packed shard. A packed shard lists its requests by request shard, then by request index, and packs their tokens in that order from slot 0. In that order the requests of a packed shard form pairs whose lengths sum to 8, so every packed shard holds exactly 256 tokens; every packed shard has a request of length 1 and one of length 7.
All inputs are finite; a program needn't handle non-finite values.
Results may differ from a plain program's by a relative error of at most 0.0003.
Values may be sent and summed in bfloat16 or wider, within the bound.
No kernel may reach another device: no remote copies, remote signals or barrier semaphores. Data moves between devices by JAX's collectives and lax.ppermute only.
A program may use at most 192 MiB of HBM per device.

v0:
```python
import jax
import jax.numpy as jnp
from jax import lax
from jax.sharding import PartitionSpec as P

kl_coef = 0.1
discount = 0.99
gae_mix = 0.95
norm_eps = 1e-05


def pair_rank(dest):
    count = dest.shape[-1]
    idx = jnp.arange(count, dtype=jnp.int32)
    same = dest[..., None, :] == dest[..., :, None]
    earlier = idx[None, :] < idx[:, None]
    return jnp.sum(jnp.logical_and(same, earlier).astype(jnp.int32), axis=-1)


def body(
    token_ids,
    lengths,
    pack_dest,
    ref_hidden,
    reward_hidden,
    head_weight,
    norm_gain,
    score_weight,
    value_weight,
    old_logprob,
):
    shards = lax.axis_size("dp")
    ways = lax.axis_size("mp")
    me = lax.axis_index("dp")
    part = lax.axis_index("mp")
    req_dev, max_len, width_dev = ref_hidden.shape
    pair_len = max_len + 1
    slot_dev = shards * pair_len
    sub_len = slot_dev // ways
    blocks = sub_len // pair_len
    width_full = width_dev * ways
    steps = jnp.arange(max_len, dtype=jnp.int32)
    dest = lax.dynamic_slice_in_dim(pack_dest, me * req_dev, req_dev)
    size = lax.dynamic_slice_in_dim(lengths, me * req_dev, req_dev)
    rank = pair_rank(dest)
    row = dest[:, None] * pair_len + steps[None, :] + rank[:, None] * (pair_len - size[:, None])
    row = jnp.where(steps[None, :] < size[:, None], row, -1).reshape(-1)
    onehot = (row[None, :] == jnp.arange(slot_dev, dtype=jnp.int32)[:, None]).astype(jnp.bfloat16)
    ref_send = jnp.dot(
        onehot, ref_hidden.reshape(req_dev * max_len, width_dev), preferred_element_type=jnp.float32
    ).astype(jnp.bfloat16)
    reward_send = jnp.dot(
        onehot,
        reward_hidden.reshape(req_dev * max_len, width_dev),
        preferred_element_type=jnp.float32,
    ).astype(jnp.bfloat16)
    send = jnp.concatenate([ref_send, reward_send], axis=1).reshape(shards, pair_len, 2 * width_dev)
    got = lax.all_to_all(send, "dp", 0, 0, tiled=True).reshape(slot_dev, 2 * width_dev)
    ref_packed = got[:, :width_dev]
    reward_packed = got[:, width_dev:]
    own_rows = lax.all_to_all(
        ref_packed.reshape(ways, sub_len, width_dev), "mp", 0, 2, tiled=True
    ).reshape(sub_len, width_full)
    block_rows = lax.all_gather(own_rows, "dp", axis=0, tiled=True)
    weight = lax.all_gather(head_weight, "mp", axis=0, tiled=True)
    first_src = part * blocks
    dest4 = lax.dynamic_slice_in_dim(pack_dest, first_src * req_dev, blocks * req_dev).reshape(
        blocks, req_dev
    )
    size4 = lax.dynamic_slice_in_dim(lengths, first_src * req_dev, blocks * req_dev).reshape(
        blocks, req_dev
    )
    tok4 = lax.dynamic_slice_in_dim(token_ids, first_src * req_dev, blocks * req_dev, axis=0)
    rank4 = pair_rank(dest4)
    key = (
        dest4[:, :, None] * sub_len
        + jnp.arange(blocks, dtype=jnp.int32)[:, None, None] * pair_len
        + steps[None, None, :]
        + rank4[:, :, None] * (pair_len - size4[:, :, None])
    )
    key = jnp.where(steps[None, None, :] < size4[:, :, None], key, -1).reshape(-1)
    hits = key[None, :] == jnp.arange(shards * sub_len, dtype=jnp.int32)[:, None]
    targets = jnp.sum(jnp.where(hits, tok4.reshape(-1)[None, :], 0), axis=1)
    logits = jnp.dot(block_rows, weight, preferred_element_type=jnp.float32)
    vocab_dev = head_weight.shape[1]
    row_max = jnp.max(logits, axis=1)
    exp_total = jnp.sum(jnp.exp(logits - row_max[:, None]), axis=1)
    column = jnp.arange(vocab_dev, dtype=jnp.int32)[None, :] + me * vocab_dev
    target_logit = jnp.sum(jnp.where(column == targets[:, None], logits, 0.0), axis=1)
    stats = jnp.stack([row_max, exp_total, target_logit]).reshape(3, shards, sub_len)
    stats = lax.all_to_all(stats, "dp", 1, 1, tiled=True)
    joint_max = jnp.max(stats[0], axis=0)
    joint_total = jnp.sum(stats[1] * jnp.exp(stats[0] - joint_max[None, :]), axis=0)
    joint_target = jnp.sum(stats[2], axis=0)
    block_logprob = joint_target - joint_max - jnp.log(joint_total)
    ref_logprob = lax.all_gather(block_logprob, "mp", axis=0, tiled=True)
    hidden_f = reward_packed.astype(jnp.float32)
    sums = jnp.stack(
        [
            jnp.sum(hidden_f * hidden_f, axis=1),
            jnp.sum(hidden_f * (norm_gain * score_weight), axis=1),
            jnp.sum(hidden_f * (norm_gain * value_weight), axis=1),
        ]
    )
    squares, score_dot, value_dot = lax.psum(sums, "mp")
    inv_rms = lax.rsqrt(squares / width_full + norm_eps)
    score = score_dot * inv_rms
    value_est = value_dot * inv_rms
    mine = (pack_dest.reshape(shards, req_dev) == me).astype(jnp.int32)
    is_first = jnp.logical_and(mine == 1, jnp.cumsum(mine, axis=1) == 1)
    first_len = jnp.sum(jnp.where(is_first, lengths.reshape(shards, req_dev), 0), axis=1)
    place = jnp.arange(pair_len, dtype=jnp.int32)[None, :]
    is_last = jnp.logical_or(place == first_len[:, None] - 1, place == pair_len - 1)
    is_last_flat = is_last.reshape(-1)
    reward = -kl_coef * (old_logprob - ref_logprob) + jnp.where(is_last_flat, score, 0.0)
    next_value = jnp.concatenate([value_est[1:], jnp.zeros((1,), jnp.float32)])
    not_last = 1.0 - is_last_flat.astype(jnp.float32)
    td_error = (reward + discount * next_value * not_last - value_est).reshape(shards, pair_len)
    decay = discount * gae_mix
    carry = td_error[:, pair_len - 1]
    columns = [carry]
    for step in range(pair_len - 2, -1, -1):
        carry = td_error[:, step] + decay * jnp.where(is_last[:, step], 0.0, carry)
        columns.append(carry)
    advantage = jnp.stack(columns[::-1], axis=1).reshape(-1)
    return (ref_logprob, advantage)


def solution(mesh):
    return jax.shard_map(
        body,
        mesh=mesh,
        in_specs=(
            P(),
            P(),
            P(),
            P("dp", None, "mp"),
            P("dp", None, "mp"),
            P("mp", "dp"),
            P("mp"),
            P("mp"),
            P("mp"),
            P("dp"),
        ),
        out_specs=(P("dp"), P("dp")),
        check_vma=False,
    )
```

profile of v0, /device:TPU:1, one launch (start us, length us, event | category | flops | bytes accessed | tf_op | source)
XLA Modules:
  0.0 304.3 jit_solution(12371459190618607233)
XLA Ops:
  7.3 0.8 broadcast_multiply_fusion
  8.2 0.8 subtract_multiply_fusion.1
  9.3 1.3 copy.33
  10.7 1.3 copy.34
  12.2 0.3 convolution_convert_fusion.1
  12.5 0.3 convolution_convert_fusion
  12.9 27.9 %all_to_all.25 = bf16[32,8,1024]{2,1,0:T(8,128)(2,1)S(1)} all-to-all(bf16[32,8,1024]{2,1,0:T(8,128)(2,1)S(1)} %maximum_bitcast_fusion), channel_id=1, replica_groups=mesh['dp'=32,'mp'=8] {'dp'}, dimensions={0} | all-to-all | bytes 1048576 | tf_op jit(solution)/shard_map/all_to_all | solution.py:58
  40.8 13.2 %all_to_all.26 = bf16[8,32,512]{2,1,0:T(8,128)(2,1)S(1)} all-to-all(bf16[8,32,512]{2,1,0:T(8,128)(2,1)S(1)} %bitcast.31), channel_id=1, replica_groups=mesh['dp'=32,'mp'=8] {'mp'}, dimensions={0} | all-to-all | bytes 524288 | tf_op jit(solution)/shard_map/all_to_all | solution.py:61
  54.0 0.7 copy.39
  54.8 0.7 all-gather.5.cloned.1.call-update
  56.0 0.2 reduce_window_sum.11
  56.9 0.2 convert_reduce_fusion
  57.6 0.6 dynamic-slice
  58.9 0.8 select_reduce_fusion.1
  59.7 0.2 fusion
  59.9 86.8 %all-gather.3.cloned.1.call-done = bf16[1024,4096]{1,0:T(8,128)(2,1)} async-done(((bf16[32,4096]{1,0:T(8,128)(2,1)}), bf16[1024,4096]{1,0:T(8,128)(2,1)}) %all-gather.3.cloned.1.call-update) | async-done | bytes 8388624 | tf_op jit(solution)/shard_map/all_gather | solution.py:64
  146.7 87.6 %all-gather.5.cloned.1.call-done = bf16[4096,2048]{1,0:T(8,128)(2,1)} async-done(((bf16[512,2048]{1,0:T(8,128)(2,1)}), bf16[4096,2048]{1,0:T(8,128)(2,1)}) %all-gather.5.cloned.1.call-update) | async-done | bytes 16777232 | tf_op jit(solution)/shard_map/all_gather | solution.py:65
  234.3 24.2 %fusion.12 = (f32[1024]{0:T(1024)S(1)}, f32[1024,2048]{1,0:T(8,128)}) fusion(bf16[1024,4096]{1,0:T(8,128)(2,1)} %all-gather.3.cloned.1.call-done, bf16[4096,2048]{1,0:T(8,128)(2,1)} %all-gather.5.cloned.1.call-done), kind=kOutput, calls=%fused_computation.58 | convolution fusion | flops 17181966336 | bytes 33558528 | tf_op jit(solution)/shard_map/dot_general | solution.py:84
  258.6 4.7 %exponential_reduce_fusion = (f32[1024]{0:T(1024)S(1)}, f32[1024]{0:T(1024)S(1)}) fusion(f32[1024,2048]{1,0:T(8,128)} %get-tuple-element.29, f32[1024]{0:T(1024)S(1)} %get-tuple-element.28, s32[1024]{0:T(1024)S(1)} %select_reduce_fusion.1, s32[2048]{0:T(1024)S(1)} %iota_add_fusion), kind=kLoop, calls=%fused_computation.1 | loop fusion | flops 10483712 | bytes 8413184 | tf_op jit(solution)/shard_map/reduce_sum | solution.py:87
  263.4 0.7 pad_maximum_fusion
  264.1 9.5 %all-to-all-start.2 = ((f32[3,32,32]{2,0,1:T(4,128)}), f32[3,32,32]{2,0,1:T(4,128)S(1)}, u32[]{:S(2)}, u32[]{:S(2)}) async-start(f32[3,32,32]{2,0,1:T(4,128)} %pad_maximum_fusion), calls=%async_computation.2 | async-start | bytes 131072 | tf_op jit(solution)/shard_map/all_to_all | solution.py:91
  273.6 8.9 %all-to-all-done.2 = f32[3,32,32]{2,0,1:T(4,128)S(1)} async-done(((f32[3,32,32]{2,0,1:T(4,128)}), f32[3,32,32]{2,0,1:T(4,128)S(1)}, u32[]{:S(2)}, u32[]{:S(2)}) %all-to-all-start.2) | async-done | bytes 12320 | tf_op jit(solution)/shard_map/all_to_all | solution.py:91
  282.7 13.6 %all-reduce.1 = (f32[256]{0:T(256)S(1)}, f32[3,256]{1,0:T(4,128)S(1)}) all-reduce(f32[256]{0:T(256)S(1)} %subtract_dynamic-update-slice_fusion, f32[3,256]{1,0:T(4,128)S(1)} %pad_maximum_fusion.1), channel_id=1, replica_groups=mesh['dp'=32,'mp'=8] {'mp'}, use_global_device_ids=true, to_apply=%add | all-reduce | flops 1024 | bytes 8192
  296.8 0.7 reshape.228
  (65 shorter events, 3.5 us)
Async XLA Ops:
  7.2 49.3 %copy-start = (s32[2048,7]{0,1:T(8,128)S(1)}, s32[2048,7]{0,1:T(8,128)}, u32[]{:S(2)}) copy-start(s32[2048,7]{0,1:T(8,128)} %param.10) | copy-start | bytes 172036
  7.2 50.4 %copy-start.8 = (u32[256]{0:T(256)S(1)}, u32[256]{0:T(256)}, u32[]{:S(2)}) copy-start(u32[256]{0:T(256)} %constant.56) | copy-start | bytes 3076
  7.2 48.4 %copy-start.2 = (s32[2048]{0:T(1024)S(1)}, s32[2048]{0:T(1024)}, u32[]{:S(2)}) copy-start(s32[2048]{0:T(1024)} %param.12) | copy-start | bytes 24580
  7.2 48.3 %copy-start.1 = (s32[2048]{0:T(1024)S(1)}, s32[2048]{0:T(1024)}, u32[]{:S(2)}) copy-start(s32[2048]{0:T(1024)} %param.11) | copy-start | bytes 24580
  7.2 51.6 %copy-start.5 = (f32[512]{0:T(512)S(1)}, f32[512]{0:T(512)}, u32[]{:S(2)}) copy-start(f32[512]{0:T(512)} %param.18) | copy-start | bytes 6148
  7.2 51.6 %copy-start.4 = (f32[512]{0:T(512)S(1)}, f32[512]{0:T(512)}, u32[]{:S(2)}) copy-start(f32[512]{0:T(512)} %param.17) | copy-start | bytes 6148
  7.2 51.6 %copy-start.3 = (f32[512]{0:T(512)S(1)}, f32[512]{0:T(512)}, u32[]{:S(2)}) copy-start(f32[512]{0:T(512)} %param.16) | copy-start | bytes 6148
  7.2 139.5 %all-gather.3.cloned.1.call-start = ((), (), s32[]{:S(2)}) async-start(), calls=%async_computation.3 | async-start | bytes 8650752 | tf_op jit(solution)/shard_map/all_gather | solution.py:64
  54.7 179.6 %all-gather.5.cloned.1.call-start = ((), (), s32[]{:S(2)}) async-start(), calls=%async_computation.4 | async-start | bytes 18874368 | tf_op jit(solution)/shard_map/all_gather | solution.py:65
  258.5 37.9 %copy-start.6 = (f32[256]{0:T(256)S(1)}, f32[256]{0:T(256)}, u32[]{:S(2)}) copy-start(f32[256]{0:T(256)} %param.19) | copy-start | bytes 3076
  264.1 18.4 %all-to-all-start.2 = ((f32[3,32,32]{2,0,1:T(4,128)}), f32[3,32,32]{2,0,1:T(4,128)S(1)}, u32[]{:S(2)}, u32[]{:S(2)}) async-start(f32[3,32,32]{2,0,1:T(4,128)} %pad_maximum_fusion), calls=%async_computation.2 | async-start | bytes 131072 | tf_op jit(solution)/shard_map/all_to_all | solution.py:91
  296.3 1.2 copy-start.7
Sparse Core Ops, SparseCore 0:
  54.8 91.8 all-gather.2
  148.6 85.6 all-gather.4
where the time goes:
time: 305 us; the launch traced here: 304 us
  waiting for transfers between devices  184 us (60%)
  blocking collectives  54.7 us (18%)
  matrix products  24.8 us (8%)
  between operations  15 us (5%)
  starting transfers between devices  9.61 us (3%)
  other arithmetic  9.59 us (3%)
  local copies, waits for them, and re-layouts  6.68 us (2%)
    all_gather x1, waiting for transfers between devices, body(): weight = lax.all_gather(head_weight, 'mp', axis=0, tiled=True)  87.6 us
    all_gather x1, waiting for transfers between devices, body(): block_rows = lax.all_gather(own_rows, 'dp', axis=0, tiled=True)  86.8 us
    all_to_all x1, blocking collectives, body(): lax.all_to_all(send, 'dp', 0, 0, tiled=True)  27.9 us
    dot_general x1, matrix products, body(): logits = jnp.dot(block_rows, weight, preferred_element_type=jnp.float32)  24.2 us
    unnamed x1, blocking collectives  13.6 us
    all_to_all x1, blocking collectives, body(): lax.all_to_all(ref_packed.reshape(ways, sub_len, width_dev), 'mp', 0, 2,...  13.2 us
    all_to_all x1, starting transfers between devices, body(): stats = lax.all_to_all(stats, 'dp', 1, 1, tiled=True)  9.53 us
    all_to_all x1, waiting for transfers between devices, body(): stats = lax.all_to_all(stats, 'dp', 1, 1, tiled=True)  8.86 us
  transfers between devices with their start and end apart: 3, of which 3 were waited for; matrix products, arithmetic and copies ran while one was open for 1% of the time, Pallas kernels for 0%

commit v1 on v0

--- a/solution.py
+++ b/solution.py
@@ -62,7 +62,34 @@
         ref_packed.reshape(ways, sub_len, width_dev), "mp", 0, 2, tiled=True
     ).reshape(sub_len, width_full)
     block_rows = lax.all_gather(own_rows, "dp", axis=0, tiled=True)
-    weight = lax.all_gather(head_weight, "mp", axis=0, tiled=True)
+
+    def _scan_strips_all(my_tile):
+        chip_axis = "mp"
+        aux, formed, found_now = (
+            lax.axis_size(chip_axis),
+            lax.axis_index(chip_axis),
+            my_tile.shape[0],
+        )
+        table = [dev_i * aux if q == 0 else dev_i for q, dev_i in enumerate(my_tile.shape)]
+        high = k_now = my_tile
+        p = 1
+        tmp = lax.dynamic_update_slice_in_dim(
+            jnp.zeros(table, my_tile.dtype), my_tile, formed * found_now, axis=0
+        )
+        while p < aux // 2 + 1:
+            high = lax.ppermute(high, chip_axis, [(q, (q + 1) % aux) for q in range(aux)])
+            tmp = lax.dynamic_update_slice_in_dim(tmp, high, (formed - p) % aux * found_now, axis=0)
+            if 2 * p < aux:
+                k_now = lax.ppermute(
+                    k_now, axis_name=chip_axis, perm=[(q, (q - 1) % aux) for q in range(aux)]
+                )
+                tmp = lax.dynamic_update_slice_in_dim(
+                    tmp, k_now, (formed + p) % aux * found_now, axis=0
+                )
+            p += 1
+        return tmp
+
+    weight = _scan_strips_all(head_weight)
     first_src = part * blocks
     dest4 = lax.dynamic_slice_in_dim(pack_dest, first_src * req_dev, blocks * req_dev).reshape(
         blocks, req_dev

time: 305 us -> 232 us (0.76)
  waiting for transfers between devices: 184 us -> 65.8 us
  local copies, waits for them, and re-layouts: 6.68 us -> 35.7 us
  starting transfers between devices: 9.61 us -> 17.6 us
  blocking collectives: 54.7 us -> 61.6 us
    all_gather x1 -> x0, waiting for transfers between devices: 87.6 us -> none  [body(): weight = lax.all_gather(head_weight, 'mp', axis=0, tiled=True)]
    all_gather x1, waiting for transfers between devices: 86.8 us -> 0.01 us  [body(): block_rows = lax.all_gather(own_rows, 'dp', axis=0, tiled=True)]
    ppermute x0 -> x7, waiting for transfers between devices: none -> 57 us  [the longest x4 56.7 us: _scan_strips_all(): lax.ppermute(high, chip_axis, [(q, (q + 1) % aux) for q in range(aux)])]
    dynamic_update_slice x0 -> x8, local copies, waits for them, and re-layouts: none -> 22.3 us  [the longest x4 11.1 us: _scan_strips_all(): lax.dynamic_update_slice_in_dim(tmp, high, (formed - p) % aux * found_now...]
    ppermute x0 -> x7, starting transfers between devices: none -> 13.1 us  [the longest x4 8.77 us: _scan_strips_all(): lax.ppermute(high, chip_axis, [(q, (q + 1) % aux) for q in range(aux)])]
    unnamed x1, blocking collectives: 13.6 us -> 20.5 us
    broadcast_in_dim x0 -> x1, local copies, waits for them, and re-layouts: none -> 6.02 us  [_scan_strips_all(): jnp.zeros(table, my_tile.dtype)]
    all_to_all x1, starting transfers between devices: 9.53 us -> 4.38 us  [body(): stats = lax.all_to_all(stats, 'dp', 1, 1, tiled=True)]
  transfers between devices with their start and end apart: 3 -> 9, of which waited for: 3 -> 6; matrix products, arithmetic and copies ran while one was open for 1% -> 14% of each run, Pallas kernels for 0% -> 0%
where the time goes in v1:
time: 232 us; the launch traced here: 231 us
  waiting for transfers between devices  65.8 us (28%)
  blocking collectives  61.6 us (27%)
  local copies, waits for them, and re-layouts  35.7 us (15%)
  matrix products  25.8 us (11%)
  starting transfers between devices  17.6 us (8%)
  between operations  15.1 us (7%)
  other arithmetic  9.71 us (4%)
    ppermute x4, waiting for transfers between devices, _scan_strips_all(): lax.ppermute(high, chip_axis, [(q, (q + 1) % aux) for q in range(aux)])  56.7 us
    all_to_all x1, blocking collectives, body(): lax.all_to_all(send, 'dp', 0, 0, tiled=True)  27.9 us
    dot_general x1, matrix products, body(): logits = jnp.dot(block_rows, weight, preferred_element_type=jnp.float32)  24.2 us
    unnamed x1, blocking collectives  20.5 us
    all_to_all x1, blocking collectives, body(): lax.all_to_all(ref_packed.reshape(ways, sub_len, width_dev), 'mp', 0, 2,...  13.2 us
    dynamic_update_slice x4, local copies, waits for them, and re-layouts, _scan_strips_all(): lax.dynamic_update_slice_in_dim(tmp, high, (formed - p) % aux * found_now...  11.1 us
    dynamic_update_slice x3, local copies, waits for them, and re-layouts, _scan_strips_all(): lax.dynamic_update_slice_in_dim(tmp, k_now, (formed + p) % aux * found_no...  9.62 us
    all_to_all x1, waiting for transfers between devices, body(): stats = lax.all_to_all(stats, 'dp', 1, 1, tiled=True)  8.8 us
  transfers between devices with their start and end apart: 9, of which 6 were waited for; matrix products, arithmetic and copies ran while one was open for 14% of the time, Pallas kernels for 0%

profile of v1, /device:TPU:1, one launch (start us, length us, event | category | flops | bytes accessed | tf_op | source)
XLA Modules:
  0.0 231.3 jit_solution(8120368279451345760)
XLA Ops:
  14.8 27.9 %all_to_all.25 = bf16[32,8,1024]{2,1,0:T(8,128)(2,1)S(1)} all-to-all(bf16[32,8,1024]{2,1,0:T(8,128)(2,1)S(1)} %maximum_bitcast_fusion), channel_id=1, replica_groups=mesh['dp'=32,'mp'=8] {'dp'}, dimensions={0} | all-to-all | bytes 1048576 | tf_op jit(solution)/shard_map/all_to_all | solution.py:58
  42.7 13.2 %all_to_all.26 = bf16[8,32,512]{2,1,0:T(8,128)(2,1)S(1)} all-to-all(bf16[8,32,512]{2,1,0:T(8,128)(2,1)S(1)} %bitcast.31), channel_id=1, replica_groups=mesh['dp'=32,'mp'=8] {'mp'}, dimensions={0} | all-to-all | bytes 524288 | tf_op jit(solution)/shard_map/all_to_all | solution.py:61
  57.9 23.0 %collective-permute-done = bf16[512,2048]{1,0:T(8,128)(2,1)S(1)} collective-permute-done((bf16[512,2048]{1,0:T(8,128)(2,1)S(1)}, bf16[512,2048]{1,0:T(8,128)(2,1)S(1)}, u32[]{:S(2)}, u32[]{:S(2)}) %collective-permute-start) | collective-permute-done | bytes 2097184 | tf_op jit(solution)/shard_map/ppermute | solution.py:80
  80.8 2.5 %collective-permute-start.2 = (bf16[512,2048]{1,0:T(8,128)(2,1)S(1)}, bf16[512,2048]{1,0:T(8,128)(2,1)}, u32[]{:S(2)}, u32[]{:S(2)}) collective-permute-start(bf16[512,2048]{1,0:T(8,128)(2,1)S(1)} %collective-permute-done), channel_id=1, source_target_pairs={{0,1},{1,2},{2,3},{3,4},{4,5},{5,6},{6,7},{7,0},{8,9},{9,10},{10,1... | collective-permute-start | bytes 6291464 | tf_op jit(solution)/shard_map/ppermute | solution.py:80
  83.6 2.1 collective-permute-start.3
  85.7 20.6 %collective-permute-done.2 = bf16[512,2048]{1,0:T(8,128)(2,1)} collective-permute-done((bf16[512,2048]{1,0:T(8,128)(2,1)S(1)}, bf16[512,2048]{1,0:T(8,128)(2,1)}, u32[]{:S(2)}, u32[]{:S(2)}) %collective-permute-start.2) | collective-permute-done | bytes 2097184 | tf_op jit(solution)/shard_map/ppermute | solution.py:80
  106.3 2.6 %collective-permute-start.4 = (bf16[512,2048]{1,0:T(8,128)(2,1)}, bf16[512,2048]{1,0:T(8,128)(2,1)}, u32[]{:S(2)}, u32[]{:S(2)}) collective-permute-start(bf16[512,2048]{1,0:T(8,128)(2,1)} %collective-permute-done.2), channel_id=1, source_target_pairs={{0,1},{1,2},{2,3},{3,4},{4,5},{5,6},{6,7},{7,0},{8,9},{9,10},{10,1... | collective-permute-start | bytes 6291464 | tf_op jit(solution)/shard_map/ppermute | solution.py:80
  110.4 2.3 collective-permute-start.5
  112.6 6.0 %broadcast_in_dim.46 = bf16[4096,2048]{1,0:T(8,128)(2,1)} broadcast(bf16[]{:T(256)} %constant.84.clone.1), dimensions={} | broadcast | bytes 16777218 | tf_op jit(solution)/shard_map/broadcast_in_dim | solution.py:77
  118.7 1.5 constant_dynamic-update-slice_fusion.7
  120.2 12.0 %collective-permute-done.4 = bf16[512,2048]{1,0:T(8,128)(2,1)} collective-permute-done((bf16[512,2048]{1,0:T(8,128)(2,1)}, bf16[512,2048]{1,0:T(8,128)(2,1)}, u32[]{:S(2)}, u32[]{:S(2)}) %collective-permute-start.4) | collective-permute-done | bytes 2097184 | tf_op jit(solution)/shard_map/ppermute | solution.py:80
  132.2 2.5 %collective-permute-start.6 = (bf16[512,2048]{1,0:T(8,128)(2,1)}, bf16[512,2048]{1,0:T(8,128)(2,1)S(1)}, u32[]{:S(2)}, u32[]{:S(2)}) collective-permute-start(bf16[512,2048]{1,0:T(8,128)(2,1)} %collective-permute-done.4), channel_id=1, source_target_pairs={{0,1},{1,2},{2,3},{3,4},{4,5},{5,6},{6,7},{7,0},{8,9},{9,10},{10,1... | collective-permute-start | bytes 6291464 | tf_op jit(solution)/shard_map/ppermute | solution.py:80
  137.6 3.2 %constant_dynamic-update-slice_fusion.6 = bf16[4096,2048]{1,0:T(8,128)(2,1)} fusion(bf16[4096,2048]{1,0:T(8,128)(2,1)} %constant_dynamic-update-slice_fusion.7, bf16[512,2048]{1,0:T(8,128)(2,1)} %copy-done.2, s32[]{:T(128)S(6)} %select_n.157), kind=kLoop, calls=%fused_computation.46 | loop fusion | bytes 4194308 | tf_op jit(solution)/shard_map/dynamic_update_slice | solution.py:81
  140.8 3.2 %constant_dynamic-update-slice_fusion.5 = bf16[4096,2048]{1,0:T(8,128)(2,1)} fusion(bf16[4096,2048]{1,0:T(8,128)(2,1)} %constant_dynamic-update-slice_fusion.6, bf16[512,2048]{1,0:T(8,128)(2,1)} %collective-permute-done.1, s32[]{:T(128)S(6)} %select_n.159), kind=kLoop, calls=%fused_computation.45 | loop fusion | bytes 4194308 | tf_op jit(solution)/shard_map/dynamic_update_slice | solution.py:86
  144.0 3.2 %constant_dynamic-update-slice_fusion.4 = bf16[4096,2048]{1,0:T(8,128)(2,1)} fusion(bf16[4096,2048]{1,0:T(8,128)(2,1)} %constant_dynamic-update-slice_fusion.5, bf16[512,2048]{1,0:T(8,128)(2,1)} %collective-permute-done.2, s32[]{:T(128)S(6)} %select_n.161), kind=kLoop, calls=%fused_computation.44 | loop fusion | bytes 4194308 | tf_op jit(solution)/shard_map/dynamic_update_slice | solution.py:81
  147.2 3.2 %constant_dynamic-update-slice_fusion.3 = bf16[4096,2048]{1,0:T(8,128)(2,1)} fusion(bf16[4096,2048]{1,0:T(8,128)(2,1)} %constant_dynamic-update-slice_fusion.4, bf16[512,2048]{1,0:T(8,128)(2,1)} %collective-permute-done.3, s32[]{:T(128)S(6)} %select_n.163), kind=kLoop, calls=%fused_computation.43 | loop fusion | bytes 4194308 | tf_op jit(solution)/shard_map/dynamic_update_slice | solution.py:86
  150.4 3.2 %constant_dynamic-update-slice_fusion.2 = bf16[4096,2048]{1,0:T(8,128)(2,1)} fusion(bf16[4096,2048]{1,0:T(8,128)(2,1)} %constant_dynamic-update-slice_fusion.3, bf16[512,2048]{1,0:T(8,128)(2,1)} %collective-permute-done.4, s32[]{:T(128)S(6)} %select_n.165), kind=kLoop, calls=%fused_computation.42 | loop fusion | bytes 4194308 | tf_op jit(solution)/shard_map/dynamic_update_slice | solution.py:81
  153.6 3.2 %constant_dynamic-update-slice_fusion.1 = bf16[4096,2048]{1,0:T(8,128)(2,1)} fusion(bf16[4096,2048]{1,0:T(8,128)(2,1)} %constant_dynamic-update-slice_fusion.2, bf16[512,2048]{1,0:T(8,128)(2,1)} %collective-permute-done.5, s32[]{:T(128)S(6)} %select_n.167), kind=kLoop, calls=%fused_computation.41 | loop fusion | bytes 4194308 | tf_op jit(solution)/shard_map/dynamic_update_slice | solution.py:86
  158.0 1.5 constant_dynamic-update-slice_fusion
  159.5 24.2 %fusion.12 = (f32[1024]{0:T(1024)S(1)}, f32[1024,2048]{1,0:T(8,128)}) fusion(bf16[1024,4096]{1,0:T(8,128)(2,1)} %all-gather.2.cloned.1.call-done, bf16[4096,2048]{1,0:T(8,128)(2,1)} %constant_dynamic-update-slice_fusion), kind=kOutput, calls=%fused_computation.66 | convolution fusion | flops 17181966336 | bytes 33558528 | tf_op jit(solution)/shard_map/dot_general | solution.py:111
  183.8 4.6 %exponential_reduce_fusion = (f32[1024]{0:T(1024)S(1)}, f32[1024]{0:T(1024)S(1)}) fusion(f32[1024,2048]{1,0:T(8,128)} %get-tuple-element.29, f32[1024]{0:T(1024)S(1)} %get-tuple-element.28, s32[1024]{0:T(1024)S(1)} %select_reduce_fusion.1, s32[2048]{0:T(1024)S(1)} %iota_add_fusion), kind=kLoop, calls=%fused_computation.1 | loop fusion | flops 10483712 | bytes 8413184 | tf_op jit(solution)/shard_map/reduce_sum | solution.py:114
  189.3 4.4 %all-to-all-start.2 = ((f32[3,32,32]{2,0,1:T(4,128)}), f32[3,32,32]{2,0,1:T(4,128)S(1)}, u32[]{:S(2)}, u32[]{:S(2)}) async-start(f32[3,32,32]{2,0,1:T(4,128)} %pad_maximum_fusion), calls=%async_computation.2 | async-start | bytes 131072 | tf_op jit(solution)/shard_map/all_to_all | solution.py:118
  193.7 8.8 %all-to-all-done.2 = f32[3,32,32]{2,0,1:T(4,128)S(1)} async-done(((f32[3,32,32]{2,0,1:T(4,128)}), f32[3,32,32]{2,0,1:T(4,128)S(1)}, u32[]{:S(2)}, u32[]{:S(2)}) %all-to-all-start.2) | async-done | bytes 12320 | tf_op jit(solution)/shard_map/all_to_all | solution.py:118
  202.7 20.5 %all-reduce.1 = (f32[256]{0:T(256)S(1)}, f32[3,256]{1,0:T(4,128)S(1)}) all-reduce(f32[256]{0:T(256)S(1)} %subtract_dynamic-update-slice_fusion, f32[3,256]{1,0:T(4,128)S(1)} %pad_maximum_fusion.1), channel_id=1, replica_groups=mesh['dp'=32,'mp'=8] {'mp'}, use_global_device_ids=true, to_apply=%add | all-reduce | flops 1024 | bytes 8192
  (89 shorter events, 16.8 us)
Async XLA Ops:
  7.2 102.4 %copy-start = (s32[2048,7]{0,1:T(8,128)S(1)}, s32[2048,7]{0,1:T(8,128)}, u32[]{:S(2)}) copy-start(s32[2048,7]{0,1:T(8,128)} %param.10) | copy-start | bytes 172036
  7.2 78.6 %copy-start.4 = (s32[2048]{0:T(1024)S(1)}, s32[2048]{0:T(1024)}, u32[]{:S(2)}) copy-start(s32[2048]{0:T(1024)} %param.12) | copy-start | bytes 24580
  7.2 101.8 %copy-start.3 = (s32[2048]{0:T(1024)S(1)}, s32[2048]{0:T(1024)}, u32[]{:S(2)}) copy-start(s32[2048]{0:T(1024)} %param.11) | copy-start | bytes 24580
  7.2 49.4 %copy-start.1 = (bf16[512,2048]{1,0:T(8,128)(2,1)S(1)}, bf16[512,2048]{1,0:T(8,128)(2,1)}, u32[]{:S(2)}) copy-start(bf16[512,2048]{1,0:T(8,128)(2,1)} %param.15) | copy-start | bytes 6291460
  7.2 102.9 %copy-start.5 = (f32[512]{0:T(512)S(1)}, f32[512]{0:T(512)}, u32[]{:S(2)}) copy-start(f32[512]{0:T(512)} %param.16) | copy-start | bytes 6148
  7.2 102.9 %copy-start.6 = (f32[512]{0:T(512)S(1)}, f32[512]{0:T(512)}, u32[]{:S(2)}) copy-start(f32[512]{0:T(512)} %param.17) | copy-start | bytes 6148
  7.2 102.9 %copy-start.7 = (f32[512]{0:T(512)S(1)}, f32[512]{0:T(512)}, u32[]{:S(2)}) copy-start(f32[512]{0:T(512)} %param.18) | copy-start | bytes 6148
  7.2 152.3 %all-gather.2.cloned.1.call-start = ((), (), s32[]{:S(2)}) async-start(), calls=%async_computation.3 | async-start | bytes 8650752 | tf_op jit(solution)/shard_map/all_gather | solution.py:64
  56.6 24.2 %collective-permute-start = (bf16[512,2048]{1,0:T(8,128)(2,1)S(1)}, bf16[512,2048]{1,0:T(8,128)(2,1)S(1)}, u32[]{:S(2)}, u32[]{:S(2)}) collective-permute-start(bf16[512,2048]{1,0:T(8,128)(2,1)S(1)} %copy-done.1), channel_id=1, source_target_pairs={{0,1},{1,2},{2,3},{3,4},{4,5},{5,6},{6,7},{7,0},{8,9},{9,10},{10,1... | collective-permute-start | bytes 6291464 | tf_op jit(solution)/shard_map/ppermute | solution.py:80
  57.9 25.8 %collective-permute-start.1 = (bf16[512,2048]{1,0:T(8,128)(2,1)S(1)}, bf16[512,2048]{1,0:T(8,128)(2,1)}, u32[]{:S(2)}, u32[]{:S(2)}) collective-permute-start(bf16[512,2048]{1,0:T(8,128)(2,1)S(1)} %copy-done.1), channel_id=1, source_target_pairs={{0,7},{1,0},{2,1},{3,2},{4,3},{5,4},{6,5},{7,6},{8,15},{9,8},{10,9... | collective-permute-start | bytes 6291464 | tf_op jit(solution)/shard_map/ppermute | solution.py:83
  80.8 2.8 %copy-start.2 = (bf16[512,2048]{1,0:T(8,128)(2,1)}, bf16[512,2048]{1,0:T(8,128)(2,1)S(1)}, u32[]{:S(2)}) copy-start(bf16[512,2048]{1,0:T(8,128)(2,1)S(1)} %collective-permute-done) | copy-start | bytes 6291460
  80.8 25.5 %collective-permute-start.2 = (bf16[512,2048]{1,0:T(8,128)(2,1)S(1)}, bf16[512,2048]{1,0:T(8,128)(2,1)}, u32[]{:S(2)}, u32[]{:S(2)}) collective-permute-start(bf16[512,2048]{1,0:T(8,128)(2,1)S(1)} %collective-permute-done), channel_id=1, source_target_pairs={{0,1},{1,2},{2,3},{3,4},{4,5},{5,6},{6,7},{7,0},{8,9},{9,10},{10,1... | collective-permute-start | bytes 6291464 | tf_op jit(solution)/shard_map/ppermute | solution.py:80
  83.6 26.8 %collective-permute-start.3 = (bf16[512,2048]{1,0:T(8,128)(2,1)}, bf16[512,2048]{1,0:T(8,128)(2,1)}, u32[]{:S(2)}, u32[]{:S(2)}) collective-permute-start(bf16[512,2048]{1,0:T(8,128)(2,1)} %collective-permute-done.1), channel_id=1, source_target_pairs={{0,7},{1,0},{2,1},{3,2},{4,3},{5,4},{6,5},{7,6},{8,15},{9,8},{10,9... | collective-permute-start | bytes 6291464 | tf_op jit(solution)/shard_map/ppermute | solution.py:83
  106.3 25.9 %collective-permute-start.4 = (bf16[512,2048]{1,0:T(8,128)(2,1)}, bf16[512,2048]{1,0:T(8,128)(2,1)}, u32[]{:S(2)}, u32[]{:S(2)}) collective-permute-start(bf16[512,2048]{1,0:T(8,128)(2,1)} %collective-permute-done.2), channel_id=1, source_target_pairs={{0,1},{1,2},{2,3},{3,4},{4,5},{5,6},{6,7},{7,0},{8,9},{9,10},{10,1... | collective-permute-start | bytes 6291464 | tf_op jit(solution)/shard_map/ppermute | solution.py:80
  110.4 25.0 %copy-start.10 = (u32[256]{0:T(256)S(1)}, u32[256]{0:T(256)}, u32[]{:S(2)}) copy-start(u32[256]{0:T(256)} %constant.108) | copy-start | bytes 3076
  110.4 43.2 %collective-permute-start.5 = (bf16[512,2048]{1,0:T(8,128)(2,1)}, bf16[512,2048]{1,0:T(8,128)(2,1)}, u32[]{:S(2)}, u32[]{:S(2)}) collective-permute-start(bf16[512,2048]{1,0:T(8,128)(2,1)} %collective-permute-done.3), channel_id=1, source_target_pairs={{0,7},{1,0},{2,1},{3,2},{4,3},{5,4},{6,5},{7,6},{8,15},{9,8},{10,9... | collective-permute-start | bytes 6291464 | tf_op jit(solution)/shard_map/ppermute | solution.py:83
  132.2 25.8 %collective-permute-start.6 = (bf16[512,2048]{1,0:T(8,128)(2,1)}, bf16[512,2048]{1,0:T(8,128)(2,1)S(1)}, u32[]{:S(2)}, u32[]{:S(2)}) collective-permute-start(bf16[512,2048]{1,0:T(8,128)(2,1)} %collective-permute-done.4), channel_id=1, source_target_pairs={{0,1},{1,2},{2,3},{3,4},{4,5},{5,6},{6,7},{7,0},{8,9},{9,10},{10,1... | collective-permute-start | bytes 6291464 | tf_op jit(solution)/shard_map/ppermute | solution.py:80
  183.7 39.7 %copy-start.8 = (f32[256]{0:T(256)S(1)}, f32[256]{0:T(256)}, u32[]{:S(2)}) copy-start(f32[256]{0:T(256)} %param.19) | copy-start | bytes 3076
  189.3 13.2 %all-to-all-start.2 = ((f32[3,32,32]{2,0,1:T(4,128)}), f32[3,32,32]{2,0,1:T(4,128)S(1)}, u32[]{:S(2)}, u32[]{:S(2)}) async-start(f32[3,32,32]{2,0,1:T(4,128)} %pad_maximum_fusion), calls=%async_computation.2 | async-start | bytes 131072 | tf_op jit(solution)/shard_map/all_to_all | solution.py:118
  223.2 1.2 copy-start.9
Sparse Core Ops, SparseCore 0:
  56.8 91.7 all-gather.1
